TPU v7x, 128 devices: a whole 4x4x4 slice. The times are simulated.
128 devices in a mesh: req: 32 (over z, y, x_lo), tp: 4 (over x_hi, core).
Axes of the slice: x: 4 (x_hi: 2, x_lo: 2; x = x_hi * 2 + x_lo), y: 4, z: 4, core: 2. Of those that a mesh axis runs over, the one named last changes fastest.
Arguments:
- tokens: bfloat16 [16384, 4096], P('req', 'tp'), may hold values from -400 to 400
- input_norm_gain: float32 [4096], replicated, may hold values from 0.1 to 1.9
- query_weight: bfloat16 [4096, 2048], P(None, 'tp'), may hold values from -0.078125 to 0.078125
- key_weight: bfloat16 [4096, 2048], P(None, 'tp'), may hold values from -1.953125 to 1.953125
- value_weight: bfloat16 [4096, 2048], P(None, 'tp'), may hold values from -0.09375 to 0.09375
- query_down_maps: bfloat16 [4096, 512], replicated, may hold values from -0.09375 to 0.09375
- value_down_maps: bfloat16 [4096, 512], replicated, may hold values from -0.09375 to 0.09375
- query_up_maps: bfloat16 [512, 2048], P(None, 'tp'), may hold values from -1.5 to 1.5
- value_up_maps: bfloat16 [512, 2048], P(None, 'tp'), may hold values from -1.5 to 1.5
- lengths: int32 [16], replicated, may hold values from 1 to 8448, 16384 in all
- prompt_adapter_index: int32 [16], replicated, may hold values from 0 to 31
Outputs:
- attended: bfloat16 [16384, 2048], P('req', 'tp')
Inputs may be any that keep to these rules, and one draw needn't show every extreme that they name: `lengths`: the longest prompt has exactly 8448 tokens.
All inputs are finite; a program needn't handle non-finite values.
Results may differ from a plain program's by a relative error of at most 0.0083.
Values may be sent and summed in bfloat16 or wider, within the bound.
No kernel may reach another device: no remote copies, remote signals or barrier semaphores. Data moves between devices by JAX's collectives and lax.ppermute only.
A program may use at most 192 MiB of HBM per device.

v0:
```python
import math

import jax
import jax.numpy as jnp
from jax import lax
from jax.sharding import PartitionSpec as P

HEAD = 128
ADAPTER_RANK = 16
ADAPTER_COUNT = 32


EPS = 1e-05
ADAPTER_SCALE = 0.5
MASKED = -1e30


def prompt_layout(lengths, positions):
    ends = jnp.cumsum(lengths)
    before = (ends[None, :] <= positions[:, None]).astype(jnp.int32)
    starts = jnp.sum(before * lengths[None, :], axis=1)
    prompt = jnp.sum(before, axis=1)
    return (starts, prompt)


def adapter_mask(prompt, prompt_adapter_index, count, rank):
    chosen = (
        prompt[:, None] == jnp.arange(prompt_adapter_index.shape[0], dtype=jnp.int32)[None, :]
    ).astype(jnp.int32)
    adapter = jnp.sum(chosen * prompt_adapter_index[None, :], axis=1)
    column = jnp.arange(count * rank, dtype=jnp.int32) // rank
    return (column[None, :] == adapter[:, None]).astype(jnp.float32)


def rotate(field, offsets, width):
    half = width // 2
    freq = jnp.exp(jnp.arange(half, dtype=jnp.float32) * (-2.0 * math.log(10000.0) / width))
    angle = offsets.astype(jnp.float32)[:, None] * freq[None, :]
    cosine = jnp.cos(angle)[:, None, :]
    sine = jnp.sin(angle)[:, None, :]
    first = field[..., :half]
    second = field[..., half:]
    return jnp.concatenate(
        [first * cosine - second * sine, second * cosine + first * sine], axis=-1
    )


def body(
    tokens,
    input_norm_gain,
    query_weight,
    key_weight,
    value_weight,
    query_down_maps,
    value_down_maps,
    query_up_maps,
    value_up_maps,
    lengths,
    prompt_adapter_index,
):
    row_count = tokens.shape[0]
    req_index = lax.axis_index("req")
    positions = req_index * row_count + jnp.arange(row_count, dtype=jnp.int32)
    starts, prompt = prompt_layout(lengths, positions)
    causal_mask = adapter_mask(prompt, prompt_adapter_index, ADAPTER_COUNT, ADAPTER_RANK)
    incoming_weights = (query_weight, key_weight, value_weight, query_down_maps, value_down_maps)
    whole = lax.all_gather(tokens, "tp", axis=1, tiled=True)
    whole_float = whole.astype(jnp.float32)
    normed = (
        whole_float
        * lax.rsqrt(jnp.mean(whole_float * whole_float, axis=1, keepdims=True) + EPS)
        * input_norm_gain[None, :]
    ).astype(jnp.bfloat16)
    projected = tuple(
        (jnp.dot(normed, weight, preferred_element_type=jnp.float32) for weight in incoming_weights)
    )
    query_linear, key_lin, value_linear, query_middle, value_middle = projected
    query_middle = (query_middle * causal_mask).astype(jnp.bfloat16)
    value_middle = (value_middle * causal_mask).astype(jnp.bfloat16)
    query_linear = query_linear + ADAPTER_SCALE * jnp.dot(
        query_middle, query_up_maps, preferred_element_type=jnp.float32
    )
    value_rows = (
        value_linear
        + ADAPTER_SCALE * jnp.dot(value_middle, value_up_maps, preferred_element_type=jnp.float32)
    ).astype(jnp.bfloat16)
    head_count = query_linear.shape[1] // HEAD
    offsets = positions - starts
    queries = jnp.transpose(
        rotate(query_linear.reshape(row_count, head_count, HEAD), offsets, HEAD).astype(
            jnp.bfloat16
        ),
        (1, 0, 2),
    )
    keys = (
        rotate(key_lin.reshape(row_count, head_count, HEAD), offsets, HEAD)
        .astype(jnp.bfloat16)
        .reshape(row_count, head_count * HEAD)
    )
    key_value = jnp.stack([keys, value_rows])
    scale = 1.0 / math.sqrt(HEAD)

    def attend(state, block, key_first):
        peak, total, summed = state
        block_rows = block.shape[1]
        key_block = block[0].reshape(block_rows, head_count, HEAD)
        value_block = block[1].reshape(block_rows, head_count, HEAD)
        scores = (
            jnp.einsum("hqd,khd->hqk", queries, key_block, preferred_element_type=jnp.float32)
            * scale
        )
        key_pos = key_first + jnp.arange(block_rows, dtype=jnp.int32)
        allowed = (key_pos[None, :] >= starts[:, None]) & (key_pos[None, :] <= positions[:, None])
        scores = jnp.where(allowed[None], scores, MASKED)
        new_peak = jnp.maximum(peak, jnp.max(scores, axis=2))
        weights = jnp.where(allowed[None], jnp.exp(scores - new_peak[:, :, None]), 0.0)
        factor = jnp.exp(peak - new_peak)
        new_total = total * factor + jnp.sum(weights, axis=2)
        new_summed = summed * factor[:, :, None] + jnp.einsum(
            "hqk,khd->hqd",
            weights.astype(jnp.bfloat16),
            value_block,
            preferred_element_type=jnp.float32,
        )
        return (new_peak, new_total, new_summed)

    def visit(state, block, key_first):
        return attend(state, block, key_first)

    initial = (
        jnp.full((head_count, row_count), MASKED, jnp.float32),
        jnp.zeros((head_count, row_count), jnp.float32),
        jnp.zeros((head_count, row_count, HEAD), jnp.float32),
    )
    piece = lax.all_gather(key_value, "req", axis=1, tiled=True)
    piece_rows = piece.shape[1]
    block_rows = row_count

    def inner(turn, carry):
        block = lax.dynamic_slice_in_dim(piece, turn * block_rows, block_rows, 1)
        return visit(carry, block, turn * block_rows)

    state = lax.fori_loop(0, piece_rows // block_rows, inner, initial)
    peak, total, summed = state
    attended = (summed / total[:, :, None]).astype(jnp.bfloat16)
    return jnp.transpose(attended, (1, 0, 2)).reshape(row_count, head_count * HEAD)


def solution(mesh):
    in_specs = (
        P("req", "tp"),
        P(),
        P(None, "tp"),
        P(None, "tp"),
        P(None, "tp"),
        P(),
        P(),
        P(None, "tp"),
        P(None, "tp"),
        P(),
        P(),
    )
    out_specs = P("req", "tp")
    return jax.shard_map(body, mesh=mesh, in_specs=in_specs, out_specs=out_specs, check_vma=False)
```

profile of v0, /device:TPU:96, one launch (start us, length us, event | category | flops | bytes accessed | tf_op | source)
XLA Modules:
  0.0 995.0 jit_solution(7347535489030912309)
XLA Ops:
  9.7 1.8 multiply_cosine_fusion
  11.5 37.3 %all-gather.3.cloned.1.call-done = bf16[512,4096]{1,0:T(8,128)(2,1)} async-done(((bf16[512,1024]{1,0:T(8,128)(2,1)}), bf16[512,4096]{1,0:T(8,128)(2,1)}) %all-gather.3.cloned.1.call-update) | async-done | bytes 4194320 | tf_op jit(solution)/shard_map/all_gather | solution.py:67
  48.8 3.2 fusion.15
  52.3 4.6 fusion.40
  56.8 6.1 fusion.18
  63.3 5.9 fusion.46
  69.7 1.3 copy.54
  73.8 7.1 fusion.44
  80.8 6.3 fusion.23
  88.6 707.8 %all-gather.5.cloned.1.call-done = bf16[2,16384,512]{2,1,0:T(8,128)(2,1)} async-done(((bf16[2,512,512]{2,1,0:T(8,128)(2,1)}), bf16[2,16384,512]{2,1,0:T(8,128)(2,1)}) %all-gather.5.cloned.1.call-update) | async-done | bytes 33554448 | tf_op jit(solution)/shard_map/all_gather | solution.py:135
  796.4 190.6 %while.18 = (s32[]{:T(128)}, f32[4,512]{1,0:T(4,128)S(1)}, f32[4,512]{1,0:T(4,128)S(1)}, f32[4,512,128]{2,1,0:T(8,128)S(1)}, s32[512]{0:T(512)S(1)}, /*index=5*/...) while((s32[]{:T(128)}, f32[4,512]{1,0:T(4,128)S(1)}, ...), condition=%wide.region_8.9_spmd.clone, body=%wide.region_5.8_spmd.clone.sunk | while | flops 552086528 | bytes 21637340 | solution.py:143
  796.7 1.3 constant_dynamic-slice_fusion.3
  800.5 1.8 fusion.76
  802.7 1.3 constant_dynamic-slice_fusion.3
  806.5 1.8 fusion.76
  808.6 1.3 constant_dynamic-slice_fusion.3
  812.4 1.8 fusion.76
  818.4 1.8 fusion.76
  820.5 1.3 constant_dynamic-slice_fusion.3
  824.3 1.8 fusion.76
  830.3 1.8 fusion.76
  836.3 1.8 fusion.76
  842.2 1.8 fusion.76
  848.2 1.8 fusion.76
  854.1 1.8 fusion.76
  860.1 1.8 fusion.76
  866.0 1.8 fusion.76
  872.0 1.8 fusion.76
  878.0 1.8 fusion.76
  883.9 1.8 fusion.76
  889.9 1.8 fusion.76
  895.8 1.8 fusion.76
  898.0 1.3 constant_dynamic-slice_fusion.3
  901.8 1.8 fusion.76
  907.8 1.8 fusion.76
  913.7 1.8 fusion.76
  919.7 1.8 fusion.76
  925.6 1.8 fusion.76
  931.6 1.8 fusion.76
  937.5 1.8 fusion.76
  943.5 1.8 fusion.76
  949.5 1.8 fusion.76
  955.4 1.8 fusion.76
  961.4 1.8 fusion.76
  967.3 1.8 fusion.76
  973.3 1.8 fusion.76
  979.2 1.8 fusion.76
  985.2 1.8 fusion.76
  (357 shorter events, 132.6 us)
Async XLA Ops:
  6.5 50.3 %copy-start = (bf16[512,512]{1,0:T(8,128)(2,1)S(1)}, bf16[512,512]{1,0:T(8,128)(2,1)}, u32[]{:S(2)}) copy-start(bf16[512,512]{1,0:T(8,128)(2,1)} %param.20) | copy-start | bytes 1572868
  6.5 45.5 %copy-start.6 = (f32[4096]{0:T(1024)S(1)}, f32[4096]{0:T(1024)}, u32[]{:S(2)}) copy-start(f32[4096]{0:T(1024)} %param.14) | copy-start | bytes 49156
  6.5 42.3 %all-gather.3.cloned.1.call-start = ((), (), s32[]{:S(2)}) async-start(), calls=%async_computation | async-start | bytes 5242880 | tf_op jit(solution)/shard_map/all_gather | solution.py:67
  7.3 789.2 %all-gather.5.cloned.1.call-start = ((), (), s32[]{:S(2)}) async-start(), calls=%async_computation.1 | async-start | bytes 34603008 | tf_op jit(solution)/shard_map/all_gather | solution.py:135
  48.8 3.4 copy-start.2
  69.7 1.9 copy-start.4
  71.0 1.2 copy-start.3
  73.8 7.1 copy-start.5
  987.0 1.2 copy-start.1
Sparse Core Ops, SparseCore 0:
  9.0 39.7 all-gather.2
  88.4 708.0 all-gather.4
where the time goes:
time: 1000 us; the launch traced here: 995 us
  waiting for transfers between devices  746 us (75%)
  matrix products  120 us (12%)
  local copies, waits for them, and re-layouts  59.4 us (6%)
  other arithmetic  53 us (5%)
  between operations  13.6 us (1%)
    all_gather x1, waiting for transfers between devices, body(): piece = lax.all_gather(key_value, 'req', axis=1, tiled=True)  708 us
    dot_general x32, matrix products, attend(): jnp.einsum('hqk,khd->hqd', weights.astype(jnp.bfloat16), value_block, pre...  58.3 us
    slice x32, local copies, waits for them, and re-layouts, attend(): value_block = block[1].reshape(block_rows, head_count, HEAD)  40.9 us
    all_gather x1, waiting for transfers between devices, body(): whole = lax.all_gather(tokens, 'tp', axis=1, tiled=True)  37.3 us
    reduce_sum x32, other arithmetic, attend(): new_total = total * factor + jnp.sum(weights, axis=2)  33.3 us
    dot_general x32, matrix products, attend(): jnp.einsum('hqd,khd->hqk', queries, key_block, preferred_element_type=jnp...  32.1 us
  transfers between devices with their start and end apart: 2, of which 2 were waited for; matrix products, arithmetic and copies ran while one was open for 0% of the time, Pallas kernels for 0%

commit v1 on v0

--- a/solution.py
+++ b/solution.py
@@ -1,3 +1,4 @@
+import functools
 import math
 
 import jax
@@ -45,7 +46,11 @@
     )
 
 
+MAXLEN = 8448
+
+
 def body(
+    req_count,
     tokens,
     input_norm_gain,
     query_weight,
@@ -59,6 +64,7 @@
     prompt_adapter_index,
 ):
     row_count = tokens.shape[0]
+    window = min(req_count - 1, -(-(MAXLEN - 1) // row_count))
     req_index = lax.axis_index("req")
     positions = req_index * row_count + jnp.arange(row_count, dtype=jnp.int32)
     starts, prompt = prompt_layout(lengths, positions)
@@ -124,23 +130,16 @@
         )
         return (new_peak, new_total, new_summed)
 
-    def visit(state, block, key_first):
-        return attend(state, block, key_first)
-
     initial = (
         jnp.full((head_count, row_count), MASKED, jnp.float32),
         jnp.zeros((head_count, row_count), jnp.float32),
         jnp.zeros((head_count, row_count, HEAD), jnp.float32),
     )
-    piece = lax.all_gather(key_value, "req", axis=1, tiled=True)
-    piece_rows = piece.shape[1]
-    block_rows = row_count
-
-    def inner(turn, carry):
-        block = lax.dynamic_slice_in_dim(piece, turn * block_rows, block_rows, 1)
-        return visit(carry, block, turn * block_rows)
-
-    state = lax.fori_loop(0, piece_rows // block_rows, inner, initial)
+    state = attend(initial, key_value, req_index * row_count)
+    for shift in range(1, window + 1):
+        pairs = [(i, i + shift) for i in range(req_count - shift)]
+        block = lax.ppermute(key_value, "req", pairs)
+        state = attend(state, block, (req_index - shift) * row_count)
     peak, total, summed = state
     attended = (summed / total[:, :, None]).astype(jnp.bfloat16)
     return jnp.transpose(attended, (1, 0, 2)).reshape(row_count, head_count * HEAD)
@@ -161,4 +160,5 @@
         P(),
     )
     out_specs = P("req", "tp")
-    return jax.shard_map(body, mesh=mesh, in_specs=in_specs, out_specs=out_specs, check_vma=False)
+    fn = functools.partial(body, mesh.shape["req"])
+    return jax.shard_map(fn, mesh=mesh, in_specs=in_specs, out_specs=out_specs, check_vma=False)

time: 1000 us -> 612 us (0.61)
  waiting for transfers between devices: 746 us -> 311 us
  starting transfers between devices: 0.04 us -> 77.9 us
  local copies, waits for them, and re-layouts: 59.4 us -> 33.6 us
    all_gather x1 -> x0, waiting for transfers between devices: 708 us -> none  [body(): piece = lax.all_gather(key_value, 'req', axis=1, tiled=True)]
    ppermute x0 -> x17, waiting for transfers between devices: none -> 278 us  [body(): block = lax.ppermute(key_value, 'req', pairs)]
    ppermute x0 -> x17, starting transfers between devices: none -> 77.9 us  [body(): block = lax.ppermute(key_value, 'req', pairs)]
    slice x32 -> x16, local copies, waits for them, and re-layouts: 40.9 us -> 20 us  [attend(): value_block = block[1].reshape(block_rows, head_count, HEAD)]
    while x96 -> x0, local copies, waits for them, and re-layouts: 13.7 us -> none
    dot_general x32 -> x18, matrix products: 58.3 us -> 53.2 us  [attend(): jnp.einsum('hqk,khd->hqd', weights.astype(jnp.bfloat16), value_block, pre...]
    reduce_sum x32 -> x9, other arithmetic: 33.3 us -> 29.8 us  [attend(): new_total = total * factor + jnp.sum(weights, axis=2)]
    dot_general x32 -> x18, matrix products: 32.1 us -> 33 us  [attend(): jnp.einsum('hqd,khd->hqk', queries, key_block, preferred_element_type=jnp...]
  transfers between devices with their start and end apart: 2 -> 18, of which waited for: 2 -> 9; matrix products, arithmetic and copies ran while one was open for 0% -> 13% of each run, Pallas kernels for 0% -> 0%
where the time goes in v1:
time: 612 us; the launch traced here: 603 us
  waiting for transfers between devices  311 us (51%)
  matrix products  118 us (19%)
  starting transfers between devices  77.9 us (13%)
  other arithmetic  47.5 us (8%)
  local copies, waits for them, and re-layouts  33.6 us (5%)
  between operations  14.8 us (2%)
    ppermute x17, waiting for transfers between devices, body(): block = lax.ppermute(key_value, 'req', pairs)  278 us
    ppermute x17, starting transfers between devices, body(): block = lax.ppermute(key_value, 'req', pairs)  77.9 us
    dot_general x18, matrix products, attend(): jnp.einsum('hqk,khd->hqd', weights.astype(jnp.bfloat16), value_block, pre...  53.2 us
    dot_general x18, matrix products, attend(): jnp.einsum('hqd,khd->hqk', queries, key_block, preferred_element_type=jnp...  33 us
    all_gather x1, waiting for transfers between devices, body(): whole = lax.all_gather(tokens, 'tp', axis=1, tiled=True)  32.3 us
    reduce_sum x9, other arithmetic, attend(): new_total = total * factor + jnp.sum(weights, axis=2)  29.8 us
    slice x16, local copies, waits for them, and re-layouts, attend(): value_block = block[1].reshape(block_rows, head_count, HEAD)  20 us
    dot_general x3, matrix products, body(): jnp.dot(normed, weight, preferred_element_type=jnp.float32)  18.6 us
  transfers between devices with their start and end apart: 18, of which 9 were waited for; matrix products, arithmetic and copies ran while one was open for 13% of the time, Pallas kernels for 0%

profile of v1, /device:TPU:96, one launch (start us, length us, event | category | flops | bytes accessed | tf_op | source)
XLA Modules:
  0.0 602.5 jit_solution(16277756172538254327)
XLA Ops:
  11.0 5.6 compare_and_fusion.17
  16.5 32.3 %all-gather.2.cloned.1.call-done = bf16[512,4096]{1,0:T(8,128)(2,1)} async-done(((bf16[512,1024]{1,0:T(8,128)(2,1)}), bf16[512,4096]{1,0:T(8,128)(2,1)}) %all-gather.2.cloned.1.call-update) | async-done | bytes 4194320 | tf_op jit(solution)/shard_map/all_gather | solution.py:73
  48.8 3.2 fusion
  52.3 4.8 fusion.374
  62.6 6.9 %fusion.372 = f32[512,512]{0,1:T(8,128)} fusion(bf16[4096,512]{1,0:T(8,128)(2,1)} %param.15, bf16[512,4096]{1,0:T(8,128)(2,1)} %all-gather.2.cloned.1.call-done, f32[4096]{0:T(1024)S(1)} %copy-done.66, f32[512]{0:T(512)S(1)} %add_rsqrt_fusion), kind=kOutput, calls=%fused_computation.393 | convolution fusion | flops 2155872256 | bytes 9455616 | tf_op jit(solution)/shard_map/dot_general | solution.py:81
  69.6 6.4 %fusion.274 = bf16[512,512]{0,1:T(8,128)(2,1)S(1)} fusion(f32[512,512]{0,1:T(8,128)} %fusion.372, bf16[512,512]{1,0:T(8,128)(2,1)S(1)} %copy-done, bf16[4096,512]{1,0:T(8,128)(2,1)} %param.17, s32[512]{0:T(512)S(1)} %add_select_fusion, s32[512]{0:T(512)S(1)} %select_reduce_fusion, bf16[512,4096]{1,0:T(8,128)(2,1)} %all-gather.2.cloned.1.call-done, ...), kind=kOutput, calls=%fused_computation.192 | convolution fusion | flops 2425880576 | bytes 10508288 | tf_op jit(solution)/shard_map/dot_general | solution.py:91
  84.0 6.9 %fusion.378 = f32[512,512]{0,1:T(8,128)} fusion(bf16[4096,512]{1,0:T(8,128)(2,1)} %param.13, bf16[512,4096]{1,0:T(8,128)(2,1)} %all-gather.2.cloned.1.call-done, f32[4096]{0:T(1024)S(1)} %copy-done.66, f32[512]{0:T(512)S(1)} %add_rsqrt_fusion), kind=kOutput, calls=%fused_computation.395 | convolution fusion | flops 2155872256 | bytes 9455616 | tf_op jit(solution)/shard_map/dot_general | solution.py:81
  90.9 6.4 %fusion.166 = f32[512,512]{0,1:T(8,128)S(1)} fusion(f32[512,512]{0,1:T(8,128)} %fusion.378, bf16[512,512]{1,0:T(8,128)(2,1)S(1)} %copy-done.65, bf16[4096,512]{1,0:T(8,128)(2,1)} %param.16, s32[512]{0:T(512)S(1)} %add_select_fusion, s32[512]{0:T(512)S(1)} %select_reduce_fusion, bf16[512,4096]{1,0:T(8,128)(2,1)} %all-gather.2.cloned.1.call-done, ...), kind=kOutput, calls=%fused_computation.152 | convolution fusion | flops 2425618432 | bytes 11032576 | tf_op jit(solution)/shard_map/dot_general | solution.py:86
  103.6 93.0 %collective-permute-done.13 = bf16[2,512,512]{1,2,0:T(8,128)(2,1)} collective-permute-done((bf16[2,512,512]{1,2,0:T(8,128)(2,1)}, bf16[2,512,512]{1,2,0:T(8,128)(2,1)}, u32[]{:S(2)}, u32[]{:S(2)}) %collective-permute-start.13) | collective-permute-done | bytes 1048608 | tf_op jit(solution)/shard_map/ppermute | solution.py:141
  203.3 2.5 collective-permute-start.6
  208.0 3.6 collective-permute-start.5
  217.6 8.7 %collective-permute-done.8 = bf16[2,512,512]{1,2,0:T(8,128)(2,1)S(1)} collective-permute-done((bf16[2,512,512]{1,2,0:T(8,128)(2,1)}, bf16[2,512,512]{1,2,0:T(8,128)(2,1)S(1)}, u32[]{:S(2)}, u32[]{:S(2)}) %collective-permute-start.8) | collective-permute-done | bytes 1048608 | tf_op jit(solution)/shard_map/ppermute | solution.py:141
  229.1 19.9 %collective-permute-done.7 = bf16[2,512,512]{1,2,0:T(8,128)(2,1)S(1)} collective-permute-done((bf16[2,512,512]{1,2,0:T(8,128)(2,1)}, bf16[2,512,512]{1,2,0:T(8,128)(2,1)S(1)}, u32[]{:S(2)}, u32[]{:S(2)}) %collective-permute-start.7) | collective-permute-done | bytes 1048608 | tf_op jit(solution)/shard_map/ppermute | solution.py:141
  251.9 50.5 %collective-permute-start.1 = (bf16[2,512,512]{1,2,0:T(8,128)(2,1)}, bf16[2,512,512]{1,2,0:T(8,128)(2,1)S(1)}, u32[]{:S(2)}, u32[]{:S(2)}) collective-permute-start(bf16[2,512,512]{1,2,0:T(8,128)(2,1)} %pad_maximum_fusion), channel_id=1, source_target_pairs={{0,8},{4,12},{8,16},{12,20},{16,24},{20,28},{24,32},{28,36},{32,40... | collective-permute-start | bytes 3145736 | tf_op jit(solution)/shard_map/ppermute | solution.py:141
  303.2 83.1 %collective-permute-done.5 = bf16[2,512,512]{1,2,0:T(8,128)(2,1)S(1)} collective-permute-done((bf16[2,512,512]{1,2,0:T(8,128)(2,1)}, bf16[2,512,512]{1,2,0:T(8,128)(2,1)S(1)}, u32[]{:S(2)}, u32[]{:S(2)}) %collective-permute-start.5) | collective-permute-done | bytes 1048608 | tf_op jit(solution)/shard_map/ppermute | solution.py:141
  402.9 2.9 fusion.11
  405.8 10.5 %collective-permute-done = bf16[2,512,512]{1,2,0:T(8,128)(2,1)S(1)} collective-permute-done((bf16[2,512,512]{1,2,0:T(8,128)(2,1)}, bf16[2,512,512]{1,2,0:T(8,128)(2,1)S(1)}, u32[]{:S(2)}, u32[]{:S(2)}) %collective-permute-start) | collective-permute-done | bytes 1048608 | tf_op jit(solution)/shard_map/ppermute | solution.py:141
  417.2 2.9 fusion.10
  420.1 2.9 fusion.9
  423.0 2.9 fusion.8
  425.9 6.7 %collective-permute-done.14 = bf16[2,512,512]{1,2,0:T(8,128)(2,1)S(1)} collective-permute-done((bf16[2,512,512]{1,2,0:T(8,128)(2,1)}, bf16[2,512,512]{1,2,0:T(8,128)(2,1)S(1)}, u32[]{:S(2)}, u32[]{:S(2)}) %collective-permute-start.14) | collective-permute-done | bytes 1048608 | tf_op jit(solution)/shard_map/ppermute | solution.py:141
  433.4 2.9 fusion.7
  436.3 2.9 fusion.6
  439.2 2.9 fusion.5
  442.1 3.5 collective-permute-done.15
  449.6 52.8 %collective-permute-done.16 = bf16[2,512,512]{1,2,0:T(8,128)(2,1)} collective-permute-done((bf16[2,512,512]{1,2,0:T(8,128)(2,1)}, bf16[2,512,512]{1,2,0:T(8,128)(2,1)}, u32[]{:S(2)}, u32[]{:S(2)}) %collective-permute-start.16) | collective-permute-done | bytes 1048608 | tf_op jit(solution)/shard_map/ppermute | solution.py:141
  504.5 2.9 fusion.20
  508.7 4.5 fusion.117
  513.2 4.6 fusion.25
  517.8 4.8 fusion.120
  522.6 4.4 fusion.123
  527.1 4.6 fusion.29
  531.7 4.7 fusion.126
  536.4 4.5 fusion.129
  540.9 4.6 fusion.33
  545.5 4.8 fusion.132
  550.3 4.5 fusion.135
  554.9 4.1 fusion.37
  559.0 3.4 fusion.138
  563.8 2.7 fusion.41
  569.2 2.7 fusion.45
  573.2 2.3 fusion.153
  575.6 2.3 fusion.49
  577.8 2.3 fusion.156
  580.1 2.3 fusion.159
  582.4 2.1 fusion.53
  585.9 2.1 fusion.21
  591.7 2.8 fusion.278
  (236 shorter events, 82.1 us)
Async XLA Ops:
  6.5 63.0 %copy-start = (bf16[512,512]{1,0:T(8,128)(2,1)S(1)}, bf16[512,512]{1,0:T(8,128)(2,1)}, u32[]{:S(2)}) copy-start(bf16[512,512]{1,0:T(8,128)(2,1)} %param.19) | copy-start | bytes 1572868
  6.5 42.3 %all-gather.2.cloned.1.call-start = ((), (), s32[]{:S(2)}) async-start(), calls=%async_computation | async-start | bytes 5242880 | tf_op jit(solution)/shard_map/all_gather | solution.py:73
  10.9 41.1 %copy-start.66 = (f32[4096]{0:T(1024)S(1)}, f32[4096]{0:T(1024)}, u32[]{:S(2)}) copy-start(f32[4096]{0:T(1024)} %param.12) | copy-start | bytes 49156
  76.0 8.0 %copy-start.34 = (bf16[512,512]{0,1:T(8,128)(2,1)}, bf16[512,512]{0,1:T(8,128)(2,1)S(1)}, u32[]{:S(2)}) copy-start(bf16[512,512]{0,1:T(8,128)(2,1)S(1)} %fusion.274) | copy-start | bytes 1572868
  77.2 13.7 %copy-start.65 = (bf16[512,512]{1,0:T(8,128)(2,1)S(1)}, bf16[512,512]{1,0:T(8,128)(2,1)}, u32[]{:S(2)}) copy-start(bf16[512,512]{1,0:T(8,128)(2,1)} %param.18) | copy-start | bytes 1572868
  77.2 119.5 %collective-permute-start.13 = (bf16[2,512,512]{1,2,0:T(8,128)(2,1)}, bf16[2,512,512]{1,2,0:T(8,128)(2,1)}, u32[]{:S(2)}, u32[]{:S(2)}) collective-permute-start(bf16[2,512,512]{1,2,0:T(8,128)(2,1)} %pad_maximum_fusion), channel_id=1, source_target_pairs={{0,56},{4,60},{8,64},{12,68},{16,72},{20,76},{24,80},{28,84},{32,8... | collective-permute-start | bytes 3145736 | tf_op jit(solution)/shard_map/ppermute | solution.py:141
  78.6 121.4 %collective-permute-start.12 = (bf16[2,512,512]{1,2,0:T(8,128)(2,1)}, bf16[2,512,512]{1,2,0:T(8,128)(2,1)}, u32[]{:S(2)}, u32[]{:S(2)}) collective-permute-start(bf16[2,512,512]{1,2,0:T(8,128)(2,1)} %pad_maximum_fusion), channel_id=1, source_target_pairs={{0,52},{4,56},{8,60},{12,64},{16,68},{20,72},{24,76},{28,80},{32,8... | collective-permute-start | bytes 3145736 | tf_op jit(solution)/shard_map/ppermute | solution.py:141
  79.9 123.4 %collective-permute-start.11 = (bf16[2,512,512]{1,2,0:T(8,128)(2,1)}, bf16[2,512,512]{1,2,0:T(8,128)(2,1)}, u32[]{:S(2)}, u32[]{:S(2)}) collective-permute-start(bf16[2,512,512]{1,2,0:T(8,128)(2,1)} %pad_maximum_fusion), channel_id=1, source_target_pairs={{0,48},{4,52},{8,56},{12,60},{16,64},{20,68},{24,72},{28,76},{32,8... | collective-permute-start | bytes 3145736 | tf_op jit(solution)/shard_map/ppermute | solution.py:141
  81.4 126.6 %collective-permute-start.10 = (bf16[2,512,512]{1,2,0:T(8,128)(2,1)}, bf16[2,512,512]{1,2,0:T(8,128)(2,1)}, u32[]{:S(2)}, u32[]{:S(2)}) collective-permute-start(bf16[2,512,512]{1,2,0:T(8,128)(2,1)} %pad_maximum_fusion), channel_id=1, source_target_pairs={{0,44},{4,48},{8,52},{12,56},{16,60},{20,64},{24,68},{28,72},{32,7... | collective-permute-start | bytes 3145736 | tf_op jit(solution)/shard_map/ppermute | solution.py:141
  82.7 130.9 %collective-permute-start.9 = (bf16[2,512,512]{1,2,0:T(8,128)(2,1)}, bf16[2,512,512]{1,2,0:T(8,128)(2,1)}, u32[]{:S(2)}, u32[]{:S(2)}) collective-permute-start(bf16[2,512,512]{1,2,0:T(8,128)(2,1)} %pad_maximum_fusion), channel_id=1, source_target_pairs={{0,40},{4,44},{8,48},{12,52},{16,56},{20,60},{24,64},{28,68},{32,7... | collective-permute-start | bytes 3145736 | tf_op jit(solution)/shard_map/ppermute | solution.py:141
  196.6 29.6 %collective-permute-start.8 = (bf16[2,512,512]{1,2,0:T(8,128)(2,1)}, bf16[2,512,512]{1,2,0:T(8,128)(2,1)S(1)}, u32[]{:S(2)}, u32[]{:S(2)}) collective-permute-start(bf16[2,512,512]{1,2,0:T(8,128)(2,1)} %pad_maximum_fusion), channel_id=1, source_target_pairs={{0,36},{4,40},{8,44},{12,48},{16,52},{20,56},{24,60},{28,64},{32,6... | collective-permute-start | bytes 3145736 | tf_op jit(solution)/shard_map/ppermute | solution.py:141
  200.0 49.1 %collective-permute-start.7 = (bf16[2,512,512]{1,2,0:T(8,128)(2,1)}, bf16[2,512,512]{1,2,0:T(8,128)(2,1)S(1)}, u32[]{:S(2)}, u32[]{:S(2)}) collective-permute-start(bf16[2,512,512]{1,2,0:T(8,128)(2,1)} %pad_maximum_fusion), channel_id=1, source_target_pairs={{0,32},{4,36},{8,40},{12,44},{16,48},{20,52},{24,56},{28,60},{32,6... | collective-permute-start | bytes 3145736 | tf_op jit(solution)/shard_map/ppermute | solution.py:141
  203.3 48.5 %collective-permute-start.6 = (bf16[2,512,512]{1,2,0:T(8,128)(2,1)}, bf16[2,512,512]{1,2,0:T(8,128)(2,1)S(1)}, u32[]{:S(2)}, u32[]{:S(2)}) collective-permute-start(bf16[2,512,512]{1,2,0:T(8,128)(2,1)} %pad_maximum_fusion), channel_id=1, source_target_pairs={{0,28},{4,32},{8,36},{12,40},{16,44},{20,48},{24,52},{28,56},{32,6... | collective-permute-start | bytes 3145736 | tf_op jit(solution)/shard_map/ppermute | solution.py:141
  208.0 178.3 %collective-permute-start.5 = (bf16[2,512,512]{1,2,0:T(8,128)(2,1)}, bf16[2,512,512]{1,2,0:T(8,128)(2,1)S(1)}, u32[]{:S(2)}, u32[]{:S(2)}) collective-permute-start(bf16[2,512,512]{1,2,0:T(8,128)(2,1)} %pad_maximum_fusion), channel_id=1, source_target_pairs={{0,24},{4,28},{8,32},{12,36},{16,40},{20,44},{24,48},{28,52},{32,5... | collective-permute-start | bytes 3145736 | tf_op jit(solution)/shard_map/ppermute | solution.py:141
  213.6 175.4 %collective-permute-start.4 = (bf16[2,512,512]{1,2,0:T(8,128)(2,1)}, bf16[2,512,512]{1,2,0:T(8,128)(2,1)S(1)}, u32[]{:S(2)}, u32[]{:S(2)}) collective-permute-start(bf16[2,512,512]{1,2,0:T(8,128)(2,1)} %pad_maximum_fusion), channel_id=1, source_target_pairs={{0,20},{4,24},{8,28},{12,32},{16,36},{20,40},{24,44},{28,48},{32,5... | collective-permute-start | bytes 3145736 | tf_op jit(solution)/shard_map/ppermute | solution.py:141
  226.3 164.9 %collective-permute-start.3 = (bf16[2,512,512]{1,2,0:T(8,128)(2,1)}, bf16[2,512,512]{1,2,0:T(8,128)(2,1)S(1)}, u32[]{:S(2)}, u32[]{:S(2)}) collective-permute-start(bf16[2,512,512]{1,2,0:T(8,128)(2,1)} %pad_maximum_fusion), channel_id=1, source_target_pairs={{0,16},{4,20},{8,24},{12,28},{16,32},{20,36},{24,40},{28,44},{32,4... | collective-permute-start | bytes 3145736 | tf_op jit(solution)/shard_map/ppermute | solution.py:141
  249.0 145.3 %collective-permute-start.2 = (bf16[2,512,512]{1,2,0:T(8,128)(2,1)}, bf16[2,512,512]{1,2,0:T(8,128)(2,1)S(1)}, u32[]{:S(2)}, u32[]{:S(2)}) collective-permute-start(bf16[2,512,512]{1,2,0:T(8,128)(2,1)} %pad_maximum_fusion), channel_id=1, source_target_pairs={{0,12},{4,16},{8,20},{12,24},{16,28},{20,32},{24,36},{28,40},{32,4... | collective-permute-start | bytes 3145736 | tf_op jit(solution)/shard_map/ppermute | solution.py:141
  251.9 141.5 %copy-start.6 = (pred[512,512]{0,1:T(8,128)(4,1)S(1)}, pred[512,512]{0,1:T(8,128)(4,1)}, u32[]{:S(2)}) copy-start(pred[512,512]{0,1:T(8,128)(4,1)} %get-tuple-element.105) | copy-start | bytes 786436
  251.9 148.2 %collective-permute-start.1 = (bf16[2,512,512]{1,2,0:T(8,128)(2,1)}, bf16[2,512,512]{1,2,0:T(8,128)(2,1)S(1)}, u32[]{:S(2)}, u32[]{:S(2)}) collective-permute-start(bf16[2,512,512]{1,2,0:T(8,128)(2,1)} %pad_maximum_fusion), channel_id=1, source_target_pairs={{0,8},{4,12},{8,16},{12,20},{16,24},{20,28},{24,32},{28,36},{32,40... | collective-permute-start | bytes 3145736 | tf_op jit(solution)/shard_map/ppermute | solution.py:141
  386.2 30.1 %collective-permute-start = (bf16[2,512,512]{1,2,0:T(8,128)(2,1)}, bf16[2,512,512]{1,2,0:T(8,128)(2,1)S(1)}, u32[]{:S(2)}, u32[]{:S(2)}) collective-permute-start(bf16[2,512,512]{1,2,0:T(8,128)(2,1)} %pad_maximum_fusion), channel_id=1, source_target_pairs={{0,4},{4,8},{8,12},{12,16},{16,20},{20,24},{24,28},{28,32},{32,36}... | collective-permute-start | bytes 3145736 | tf_op jit(solution)/shard_map/ppermute | solution.py:141
  389.0 43.5 %collective-permute-start.14 = (bf16[2,512,512]{1,2,0:T(8,128)(2,1)}, bf16[2,512,512]{1,2,0:T(8,128)(2,1)S(1)}, u32[]{:S(2)}, u32[]{:S(2)}) collective-permute-start(bf16[2,512,512]{1,2,0:T(8,128)(2,1)} %pad_maximum_fusion), channel_id=1, source_target_pairs={{0,60},{4,64},{8,68},{12,72},{16,76},{20,80},{24,84},{28,88},{32,9... | collective-permute-start | bytes 3145736 | tf_op jit(solution)/shard_map/ppermute | solution.py:141
  391.2 54.4 %collective-permute-start.15 = (bf16[2,512,512]{1,2,0:T(8,128)(2,1)}, bf16[2,512,512]{1,2,0:T(8,128)(2,1)S(1)}, u32[]{:S(2)}, u32[]{:S(2)}) collective-permute-start(bf16[2,512,512]{1,2,0:T(8,128)(2,1)} %pad_maximum_fusion), channel_id=1, source_target_pairs={{0,64},{4,68},{8,72},{12,76},{16,80},{20,84},{24,88},{28,92},{32,9... | collective-permute-start | bytes 3145736 | tf_op jit(solution)/shard_map/ppermute | solution.py:141
  393.3 3.7 copy-start.7
  394.3 3.7 copy-start.8
  394.3 108.1 %collective-permute-start.16 = (bf16[2,512,512]{1,2,0:T(8,128)(2,1)}, bf16[2,512,512]{1,2,0:T(8,128)(2,1)}, u32[]{:S(2)}, u32[]{:S(2)}) collective-permute-start(bf16[2,512,512]{1,2,0:T(8,128)(2,1)} %pad_maximum_fusion), channel_id=1, source_target_pairs={{0,68},{4,72},{8,76},{12,80},{16,84},{20,88},{24,92},{28,96},{32,1... | collective-permute-start | bytes 3145736 | tf_op jit(solution)/shard_map/ppermute | solution.py:141
  402.9 14.3 %copy-start.14 = (pred[512,512]{0,1:T(8,128)(4,1)S(1)}, pred[512,512]{0,1:T(8,128)(4,1)}, u32[]{:S(2)}) copy-start(pred[512,512]{0,1:T(8,128)(4,1)} %get-tuple-element.98) | copy-start | bytes 786436
  405.8 14.3 %copy-start.15 = (pred[512,512]{0,1:T(8,128)(4,1)S(1)}, pred[512,512]{0,1:T(8,128)(4,1)}, u32[]{:S(2)}) copy-start(pred[512,512]{0,1:T(8,128)(4,1)} %get-tuple-element.97) | copy-start | bytes 786436
  417.2 5.8 copy-start.17
  423.0 10.4 %copy-start.18 = (pred[512,512]{0,1:T(8,128)(4,1)S(1)}, pred[512,512]{0,1:T(8,128)(4,1)}, u32[]{:S(2)}) copy-start(pred[512,512]{0,1:T(8,128)(4,1)} %get-tuple-element.95) | copy-start | bytes 786436
  425.9 10.4 %copy-start.20 = (pred[512,512]{0,1:T(8,128)(4,1)S(1)}, pred[512,512]{0,1:T(8,128)(4,1)}, u32[]{:S(2)}) copy-start(pred[512,512]{0,1:T(8,128)(4,1)} %get-tuple-element.94) | copy-start | bytes 786436
  433.4 5.8 copy-start.21
  442.1 5.5 copy-start.5
  449.6 59.1 %copy-start.47 = (bf16[1,512,512]{1,2,0:T(8,128)(2,1)S(1)}, bf16[1,512,512]{1,2,0:T(8,128)(2,1)}, u32[]{:S(2)}) copy-start(bf16[1,512,512]{1,2,0:T(8,128)(2,1)} %get-tuple-element.54) | copy-start | bytes 1572868
  508.7 4.5 copy-start.62
  508.7 27.8 %copy-start.59 = (f32[4,512]{1,0:T(4,128)}, f32[4,512]{1,0:T(4,128)S(1)}, u32[]{:S(2)}) copy-start(f32[4,512]{1,0:T(4,128)S(1)} %get-tuple-element.42) | copy-start | bytes 24580
  508.7 41.6 %copy-start.58 = (f32[4,512]{1,0:T(4,128)}, f32[4,512]{1,0:T(4,128)S(1)}, u32[]{:S(2)}) copy-start(f32[4,512]{1,0:T(4,128)S(1)} %get-tuple-element.40) | copy-start | bytes 24580
  508.7 4.5 copy-start.61
  517.8 4.8 copy-start.19
  517.8 4.8 copy-start.46
  517.8 4.8 copy-start.60
  531.7 4.7 copy-start.16
  531.7 4.7 copy-start.42
  545.5 4.8 copy-start.13
  545.5 4.8 copy-start.41
  585.8 3.8 copy-start.31
  585.9 3.8 copy-start.32
  585.9 3.8 copy-start.33
  591.7 3.8 copy-start.1
  (37 other events, 77.9 us)
Sparse Core Ops, SparseCore 0:
  9.0 39.7 all-gather.1
